TPU v7x, 256 devices: a whole 4x4x8 slice. The times are simulated.
256 devices in a mesh: ctx: 8 (over y, x_hi), ch: 32 (over z, x_lo, core).
Axes of the slice: x: 4 (x_hi: 2, x_lo: 2; x = x_hi * 2 + x_lo), y: 4, z: 8, core: 2. Of those that a mesh axis runs over, the one named last changes fastest.
Arguments:
- gate_act: bfloat16 [4096, 8192], P('ctx', 'ch'), may hold values from -6 to 6
- key_act: bfloat16 [4096, 8192], P('ctx', 'ch'), may hold values from -6 to 6
- value_act: bfloat16 [4096, 8192], P('ctx', 'ch'), may hold values from -6 to 6
- filter_taps: float32 [6144, 8192], P('ctx', 'ch'), may hold values from -2 to 2
- skip_gain: float32 [8192], P('ch'), may hold values from 0.5 to 1.5
- w_out: bfloat16 [8192, 8192], P(None, 'ch'), may hold values from -0.0625 to 0.0625
- span_order: int32 [16], replicated, may hold values from 0 to 15, each once
- decode_order: int32 [8], replicated, may hold values from 0 to 7, each once
Outputs:
- projected: bfloat16 [4096, 8192], P('ctx', 'ch')
- tail: float32 [2048, 8192], P('ctx', 'ch')
Inputs may be any that keep to these rules, and one draw needn't show every extreme that they name: `span_order`: each span number once. `decode_order`: each future block number once.
All inputs are finite; a program needn't handle non-finite values.
Results may differ from a plain program's by a relative error of at most 0.017.
Values may be sent and summed in bfloat16 or wider, within the bound.
No kernel may reach another device: no remote copies, remote signals or barrier semaphores. Data moves between devices by JAX's collectives and lax.ppermute only.
A program may use at most 128 MiB of HBM per device.

v0:
```python
import math
import jax
import jax.numpy as jnp
from jax import lax
from jax.sharding import PartitionSpec as P

SPAN = 256
HIGH = lax.Precision.HIGH


def forward_table(length):
    half = length // 2
    rows_idx = lax.broadcasted_iota(jnp.int32, (length, length), 0)
    cols_idx = lax.broadcasted_iota(jnp.int32, (length, length), 1)
    frequency = rows_idx % half
    phase = (frequency * cols_idx % length).astype(jnp.float32) * (2.0 * math.pi / length)
    parity = (1 - 2 * (cols_idx % 2)).astype(jnp.float32)
    table = jnp.where(rows_idx < half, jnp.cos(phase), -jnp.sin(phase))
    return jnp.where(rows_idx == half, parity, table)


def inverse_table(length):
    half = length // 2
    rows_idx = lax.broadcasted_iota(jnp.int32, (half, length), 0)
    cols_idx = lax.broadcasted_iota(jnp.int32, (half, length), 1)
    frequency = cols_idx % half
    phase = (frequency * rows_idx % length).astype(jnp.float32) * (2.0 * math.pi / length)
    weight = jnp.where(frequency == 0, 1.0 / length, 2.0 / length)
    table = jnp.where(cols_idx < half, weight * jnp.cos(phase), -weight * jnp.sin(phase))
    parity = (1 - 2 * (rows_idx % 2)).astype(jnp.float32) / length
    return jnp.where(cols_idx == half, parity, table)


def spectral_product(left, right):
    half = left.shape[-2] // 2
    left_re, left_im = (left[..., :half, :], left[..., half:, :])
    right_re, right_im = (right[..., :half, :], right[..., half:, :])
    first = lax.broadcasted_iota(jnp.int32, left_re.shape, left_re.ndim - 2) == 0
    real_part = jnp.where(first, left_re * right_re, left_re * right_re - left_im * right_im)
    imag_part = jnp.where(first, left_im * right_im, left_re * right_im + left_im * right_re)
    return jnp.concatenate([real_part, imag_part], axis=-2)


def per_device(
    gate_act, key_act, value_act, filter_taps, skip_gain, w_out, span_order, decode_order
):
    width = gate_act.shape[1]
    length = 2 * SPAN
    cycle_size = lax.axis_size("ctx")
    position = lax.axis_index("ctx")
    count_spans = 2 * cycle_size
    count_lags = 3 * cycle_size
    forward = forward_table(length).astype(jnp.bfloat16)
    inverse = inverse_table(length)
    signal = (key_act.astype(jnp.float32) * value_act.astype(jnp.float32)).astype(jnp.bfloat16)
    all_taps = lax.all_gather(filter_taps.astype(jnp.bfloat16), "ctx", axis=0, tiled=True)
    blocks = all_taps.reshape(count_lags, SPAN, width)
    earlier = jnp.concatenate([jnp.zeros((1, SPAN, width), jnp.bfloat16), blocks[:-1]], axis=0)
    seg_spec = jnp.einsum(
        "kn,anc->akc", forward[:, :SPAN], blocks, preferred_element_type=jnp.float32
    ) + jnp.einsum(
        "kn,anc->akc", forward[:, SPAN + 1 :], earlier[:, 1:, :], preferred_element_type=jnp.float32
    )
    piece = lax.all_gather(signal, "ctx", axis=0, tiled=True)
    span_spec = jnp.einsum(
        "kn,anc->akc",
        forward[:, :SPAN],
        piece.reshape(count_spans, SPAN, width),
        preferred_element_type=jnp.float32,
    )
    my_spans = lax.dynamic_slice_in_dim(span_order, 2 * position, 2)
    my_future = count_spans + lax.dynamic_index_in_dim(decode_order, position, keepdims=False)
    targets = jnp.concatenate([my_spans, my_future[None]])
    lags = targets[:, None] - span_order[None, :]
    picked = jnp.take(seg_spec, jnp.maximum(lags, 0), axis=0)
    terms = spectral_product(picked, span_spec[None])
    totals = jnp.sum(jnp.where((lags >= 0)[:, :, None, None], terms, 0.0), axis=1)
    blocks_out = jnp.einsum(
        "nk,akc->anc", inverse, totals, precision=HIGH, preferred_element_type=jnp.float32
    )
    conv = blocks_out[:2].reshape(2 * SPAN, width)
    tail = blocks_out[2]
    mixed = (
        gate_act.astype(jnp.float32) * (conv + skip_gain[None, :] * signal.astype(jnp.float32))
    ).astype(jnp.bfloat16)
    summed = jnp.dot(
        lax.all_gather(mixed, "ch", axis=1, tiled=True), w_out, preferred_element_type=jnp.float32
    )
    projected = summed.astype(jnp.bfloat16)
    return (projected, tail)


def solution(mesh):
    in_specs = (
        P("ctx", "ch"),
        P("ctx", "ch"),
        P("ctx", "ch"),
        P("ctx", "ch"),
        P("ch"),
        P(None, "ch"),
        P(),
        P(),
    )
    out_specs = (P("ctx", "ch"), P("ctx", "ch"))
    return jax.shard_map(
        per_device, mesh=mesh, in_specs=in_specs, out_specs=out_specs, check_vma=False
    )
```

profile of v0, /device:TPU:1, one launch (start us, length us, event | category | flops | bytes accessed | tf_op | source)
XLA Modules:
  0.0 318.4 jit_solution(5243990914818297299)
XLA Ops:
  7.2 1.8 multiply_convert_fusion
  9.1 1.9 convert_element_type.55
  11.1 0.7 dynamic_slice.7
  11.8 1.2 dynamic_slice.8
  16.4 0.7 subtract_compare_fusion
  17.1 5.0 %select_convert_fusion = bf16[512,512]{1,0:T(8,128)(2,1)S(1)} fusion(s32[512]{0:T(512)S(1)} %get-tuple-element.8, s32[512]{0:T(512)S(1)} %get-tuple-element.9, s32[512]{0:T(512)S(1)} %get-tuple-element.12, s32[512]{0:T(512)S(1)} %get-tuple-element.13, pred[512]{0:T(512)(128)(4,1)S(1)} %get-tuple-element.15, pred[512]{0:T(512)(128)(4,1)S(1)} %get-tuple-element.10, ...), kind=kLoop, calls=%fused_computation.21 | loop fusion | flops 6029312 | bytes 534528 | tf_op jit(solution)/shard_map/convert_element_type | solution.py:53
  22.1 50.8 %all-gather.6.cloned.1.call-done = bf16[4096,256]{1,0:T(8,128)(2,1)} async-done(((bf16[512,256]{1,0:T(8,128)(2,1)}), bf16[4096,256]{1,0:T(8,128)(2,1)}) %all-gather.6.cloned.1.call-update) | async-done | bytes 2097168 | tf_op jit(solution)/shard_map/all_gather | solution.py:64
  72.9 2.9 convolution_bitcast_fusion
  75.8 4.2 %slice_bitcast_fusion.1 = (f32[16,256,256]{1,2,0:T(8,128)}, f32[16,256,256]{1,2,0:T(8,128)}) fusion(f32[1,16,512,256]{2,3,1,0:T(8,128)S(1)} %convolution_bitcast_fusion), kind=kLoop, calls=%fused_computation.9 | loop fusion | bytes 16777216 | tf_op jit(solution)/shard_map/mul | solution.py:39
  80.0 5.4 %copy.16 = f32[16,256,256]{2,1,0:T(8,128)} copy(f32[16,256,256]{1,2,0:T(8,128)} %get-tuple-element.4) | data formatting | bytes 8388608 | tf_op jit(solution)/shard_map/mul | solution.py:39
  85.5 5.5 %copy.17 = f32[16,256,256]{2,1,0:T(8,128)} copy(f32[16,256,256]{1,2,0:T(8,128)} %get-tuple-element.5) | data formatting | bytes 8388608 | tf_op jit(solution)/shard_map/mul | solution.py:39
  91.0 49.8 %all-gather.4.cloned.1.call-done = bf16[6144,256]{1,0:T(8,128)(2,1)} async-done(((bf16[768,256]{1,0:T(8,128)(2,1)}), bf16[6144,256]{1,0:T(8,128)(2,1)}) %all-gather.4.cloned.1.call-update) | async-done | bytes 3145744 | tf_op jit(solution)/shard_map/all_gather | solution.py:56
  140.7 8.4 %fusion.44 = f32[512,24,256]{2,0,1:T(8,128)} fusion(bf16[24,256,256]{2,1,0:T(8,128)(2,1)} %bitcast.44, bf16[512,512]{1,0:T(8,128)(2,1)S(1)} %select_convert_fusion), kind=kOutput, calls=%fused_computation.69 | convolution fusion | flops 1610612736 | bytes 15990784 | tf_op jit(solution)/shard_map/kn,anc->akc/dot_general | solution.py:59
  149.2 1.8 slice.50
  151.0 3.4 %copy.13 = bf16[23,256,256]{1,2,0:T(8,128)(2,1)S(1)} copy(bf16[23,256,256]{2,1,0:T(8,128)(2,1)} %bitcast.45) | data formatting | bytes 6029312 | tf_op jit(solution)/shard_map/slice | solution.py:58
  154.4 11.0 %bitcast_add_fusion = f32[24,512,256]{2,1,0:T(8,128)} fusion(f32[512,24,256]{2,0,1:T(8,128)} %fusion.44, bf16[23,256,256]{1,2,0:T(8,128)(2,1)S(1)} %copy.13, bf16[512,512]{1,0:T(8,128)(2,1)S(1)} %select_convert_fusion), kind=kOutput, calls=%fused_computation.4 | convolution fusion | flops 1607467008 | bytes 28442624 | tf_op jit(solution)/shard_map/kn,anc->akc/dot_general | solution.py:61
  165.4 15.2 %gather_fusion = f32[48,512,256]{2,1,0:T(8,128)} fusion(f32[24,512,256]{2,1,0:T(8,128)} %bitcast_add_fusion, s32[1024]{0:T(1024)S(1)} %pad_clamp_fusion), kind=kCustom, calls=%fused_computation | custom fusion | bytes 50331840 | tf_op jit(solution)/shard_map/jit(_take)/gather | solution.py:75
  180.7 9.8 %broadcast_select_fusion = f32[3,16,512,256]{3,2,1,0:T(8,128)S(1)} fusion(f32[3,16,512,256]{3,2,1,0:T(8,128)} %bitcast.43, pred[3,16]{1,0:T(4,128)(4,1)S(1)} %get-tuple-element.7), kind=kLoop, calls=%fused_computation.6 | loop fusion | flops 6291456 | bytes 50331696 | tf_op jit(solution)/shard_map/jit(_take)/select_n | solution.py:75
  190.5 12.4 %subtract_select_fusion = (f32[3,16,256,256]{3,2,1,0:T(8,128)}, f32[3,16,256,256]{3,2,1,0:T(8,128)}) fusion(f32[3,16,512,256]{3,2,1,0:T(8,128)S(1)} %broadcast_select_fusion, f32[16,256,256]{2,1,0:T(8,128)} %copy.17, f32[16,256,256]{2,1,0:T(8,128)} %copy.16, pred[256]{0:T(512)(128)(4,1)S(1)} %copy-done.8), kind=kLoop, calls=%fused_computation.3 | loop fusion | flops 25165824 | bytes 58720512 | tf_op jit(solution)/shard_map/jit(_where)/select_n | solution.py:39
  202.9 9.9 %fusion = f32[3,512,256]{2,1,0:T(8,128)S(1)} fusion(f32[3,16,256,256]{3,2,1,0:T(8,128)} %get-tuple-element.3, f32[3,16,256,256]{3,2,1,0:T(8,128)} %get-tuple-element.2, pred[3,16]{1,0:T(4,128)(4,1)S(1)} %get-tuple-element.6), kind=kLoop, calls=%fused_computation.2 | loop fusion | flops 18481152 | bytes 26738736 | tf_op jit(solution)/shard_map/reduce_sum | solution.py:77
  212.9 3.0 convolution_bitcast_fusion.1
  215.9 0.8 fusion.16
  217.5 86.8 %all-gather.8.cloned.1.call-done = bf16[512,8192]{1,0:T(8,128)(2,1)} async-done(((bf16[512,256]{1,0:T(8,128)(2,1)}), bf16[512,8192]{1,0:T(8,128)(2,1)}) %all-gather.8.cloned.1.call-update) | async-done | bytes 8388624 | tf_op jit(solution)/shard_map/all_gather | solution.py:87
  304.3 7.6 %convolution_convert_fusion = bf16[512,256]{1,0:T(8,128)(2,1)} fusion(bf16[512,8192]{1,0:T(8,128)(2,1)} %all-gather.8.cloned.1.call-done, bf16[8192,256]{1,0:T(8,128)(2,1)} %param.13), kind=kOutput, calls=%fused_computation.17 | convolution fusion | flops 2147614720 | bytes 12845056 | tf_op jit(solution)/shard_map/dot_general | solution.py:86
  (51 shorter events, 3.6 us)
Async XLA Ops:
  7.2 65.7 %all-gather.6.cloned.1.call-start = ((), (), s32[]{:S(2)}) async-start(), calls=%async_computation.1 | async-start | bytes 2359296 | tf_op jit(solution)/shard_map/all_gather | solution.py:64
  9.0 131.7 %all-gather.4.cloned.1.call-start = ((), (), s32[]{:S(2)}) async-start(), calls=%async_computation | async-start | bytes 3538944 | tf_op jit(solution)/shard_map/all_gather | solution.py:56
  11.0 293.3 %all-gather.8.cloned.1.call-start = ((), (), s32[]{:S(2)}) async-start(), calls=%async_computation.2 | async-start | bytes 8650752 | tf_op jit(solution)/shard_map/all_gather | solution.py:87
  15.7 64.3 %copy-start.9 = (pred[512]{0:T(512)(128)(4,1)}, pred[512]{0:T(512)(128)(4,1)S(1)}, u32[]{:S(2)}) copy-start(pred[512]{0:T(512)(128)(4,1)S(1)} %get-tuple-element.10) | copy-start | bytes 1540
  15.7 64.3 %copy-start.11 = (pred[512]{0:T(512)(128)(4,1)}, pred[512]{0:T(512)(128)(4,1)S(1)}, u32[]{:S(2)}) copy-start(pred[512]{0:T(512)(128)(4,1)S(1)} %get-tuple-element.11) | copy-start | bytes 1540
  15.7 64.3 %copy-start.13 = (pred[512]{0:T(512)(128)(4,1)}, pred[512]{0:T(512)(128)(4,1)S(1)}, u32[]{:S(2)}) copy-start(pred[512]{0:T(512)(128)(4,1)S(1)} %get-tuple-element.15) | copy-start | bytes 1540
  16.3 63.7 %copy-start.3 = (s32[512]{0:T(512)}, s32[512]{0:T(512)S(1)}, u32[]{:S(2)}) copy-start(s32[512]{0:T(512)S(1)} %get-tuple-element.9) | copy-start | bytes 6148
  140.7 8.4 %copy-start = (bf16[6144,256]{1,0:T(8,128)(2,1)S(1)}, bf16[6144,256]{1,0:T(8,128)(2,1)}, u32[]{:S(2)}) copy-start(bf16[6144,256]{1,0:T(8,128)(2,1)} %all-gather.4.cloned.1.call-done) | copy-start | bytes 9437188
  180.7 9.8 %copy-start.8 = (pred[256]{0:T(512)(128)(4,1)S(1)}, pred[256]{0:T(512)(128)(4,1)}, u32[]{:S(2)}) copy-start(pred[256]{0:T(512)(128)(4,1)} %iota_compare_fusion.2) | copy-start | bytes 772
  202.8 10.0 %copy-start.4 = (s32[512]{0:T(512)S(1)}, s32[512]{0:T(512)}, u32[]{:S(2)}) copy-start(s32[512]{0:T(512)} %copy-done.3) | copy-start | bytes 6148
  202.8 10.0 %copy-start.5 = (s32[256]{0:T(256)S(1)}, s32[256]{0:T(256)}, u32[]{:S(2)}) copy-start(s32[256]{0:T(256)} %get-tuple-element.16) | copy-start | bytes 3076
  202.8 10.0 %copy-start.6 = (s32[256]{0:T(256)S(1)}, s32[256]{0:T(256)}, u32[]{:S(2)}) copy-start(s32[256]{0:T(256)} %get-tuple-element.17) | copy-start | bytes 3076
  202.8 10.0 %copy-start.10 = (pred[512]{0:T(512)(128)(4,1)S(1)}, pred[512]{0:T(512)(128)(4,1)}, u32[]{:S(2)}) copy-start(pred[512]{0:T(512)(128)(4,1)} %copy-done.9) | copy-start | bytes 1540
  202.9 10.0 %copy-start.12 = (pred[512]{0:T(512)(128)(4,1)S(1)}, pred[512]{0:T(512)(128)(4,1)}, u32[]{:S(2)}) copy-start(pred[512]{0:T(512)(128)(4,1)} %copy-done.11) | copy-start | bytes 1540
  202.9 10.0 %copy-start.14 = (pred[512]{0:T(512)(128)(4,1)S(1)}, pred[512]{0:T(512)(128)(4,1)}, u32[]{:S(2)}) copy-start(pred[512]{0:T(512)(128)(4,1)} %copy-done.13) | copy-start | bytes 1540
  202.9 10.0 %copy-start.15 = (pred[256]{0:T(512)(128)(4,1)S(1)}, pred[256]{0:T(512)(128)(4,1)}, u32[]{:S(2)}) copy-start(pred[256]{0:T(512)(128)(4,1)} %compare_and_fusion) | copy-start | bytes 772
  202.9 13.0 %copy-start.1 = (bf16[512,256]{1,0:T(8,128)(2,1)S(1)}, bf16[512,256]{1,0:T(8,128)(2,1)}, u32[]{:S(2)}) copy-start(bf16[512,256]{1,0:T(8,128)(2,1)} %multiply_convert_fusion) | copy-start | bytes 786436
  202.9 13.0 %copy-start.2 = (bf16[512,256]{1,0:T(8,128)(2,1)S(1)}, bf16[512,256]{1,0:T(8,128)(2,1)}, u32[]{:S(2)}) copy-start(bf16[512,256]{1,0:T(8,128)(2,1)} %param.8) | copy-start | bytes 786436
  202.9 13.0 %copy-start.7 = (f32[256]{0:T(256)S(1)}, f32[256]{0:T(256)}, u32[]{:S(2)}) copy-start(f32[256]{0:T(256)} %param.12) | copy-start | bytes 3076
Sparse Core Ops, SparseCore 0:
  11.2 61.6 all-gather.5
  75.5 65.1 all-gather.3
  216.9 87.3 all-gather.7
where the time goes:
time: 319 us; the launch traced here: 318 us
  waiting for transfers between devices  187 us (59%)
  other arithmetic  44.8 us (14%)
  local copies, waits for them, and re-layouts  38.4 us (12%)
  matrix products  32.9 us (10%)
  between operations  14.7 us (5%)
    all_gather x1, waiting for transfers between devices, per_device(): lax.all_gather(mixed, 'ch', axis=1, tiled=True)  86.8 us
    all_gather x1, waiting for transfers between devices, per_device(): piece = lax.all_gather(signal, 'ctx', axis=0, tiled=True)  50.8 us
    all_gather x1, waiting for transfers between devices, per_device(): lax.all_gather(filter_taps.astype(jnp.bfloat16), 'ctx', axis=0, tiled=True)  49.8 us
    gather x1, local copies, waits for them, and re-layouts, per_device(): picked = jnp.take(seg_spec, jnp.maximum(lags, 0), axis=0)  15.2 us
    select_n x1, other arithmetic, spectral_product(): jnp.where(first, left_re * right_re, left_re * right_re - left_im * right...  12.4 us
    dot_general x1, matrix products, per_device(): jnp.einsum('kn,anc->akc', forward[:, SPAN + 1:], earlier[:, 1:, :], prefe...  11 us
    reduce_sum x1, other arithmetic, per_device(): jnp.sum(jnp.where((lags >= 0)[:, :, None, None], terms, 0.0), axis=1)  9.87 us
    select_n x1, other arithmetic, per_device(): picked = jnp.take(seg_spec, jnp.maximum(lags, 0), axis=0)  9.8 us
  transfers between devices with their start and end apart: 3, of which 3 were waited for; matrix products, arithmetic and copies ran while one was open for 10% of the time, Pallas kernels for 0%

commit v1 on v0

--- a/solution.py
+++ b/solution.py
@@ -53,7 +53,10 @@
     forward = forward_table(length).astype(jnp.bfloat16)
     inverse = inverse_table(length)
     signal = (key_act.astype(jnp.float32) * value_act.astype(jnp.float32)).astype(jnp.bfloat16)
-    all_taps = lax.all_gather(filter_taps.astype(jnp.bfloat16), "ctx", axis=0, tiled=True)
+    boxes_change = lambda x_part: jnp.concatenate(
+        lax.all_to_all(jnp.stack(lax.axis_size("ctx") * [x_part], axis=0), "ctx", 0, 0), axis=0
+    )
+    all_taps = boxes_change(filter_taps.astype(jnp.bfloat16))
     blocks = all_taps.reshape(count_lags, SPAN, width)
     earlier = jnp.concatenate([jnp.zeros((1, SPAN, width), jnp.bfloat16), blocks[:-1]], axis=0)
     seg_spec = jnp.einsum(

time: 319 us -> 243 us (0.76)
  waiting for transfers between devices: 187 us -> 122 us
  matrix products: 32.9 us -> 22.9 us
  starting transfers between devices: 0.12 us -> 7.55 us
  local copies, waits for them, and re-layouts: 38.4 us -> 33.7 us
    all_gather x1, waiting for transfers between devices: 50.8 us -> 0.01 us  [per_device(): piece = lax.all_gather(signal, 'ctx', axis=0, tiled=True)]
    all_gather x1 -> x0, waiting for transfers between devices: 49.8 us -> none  [per_device(): lax.all_gather(filter_taps.astype(jnp.bfloat16), 'ctx', axis=0, tiled=True)]
    all_to_all x0 -> x1, waiting for transfers between devices: none -> 32.4 us  [per_device(): lax.all_to_all(jnp.stack(lax.axis_size('ctx') * [x_part], axis=0), 'ctx',...]
    select_n x1, other arithmetic: 9.8 us -> 17.5 us  [per_device(): picked = jnp.take(seg_spec, jnp.maximum(lags, 0), axis=0)]
    all_to_all x0 -> x1, starting transfers between devices: none -> 7.47 us  [per_device(): lax.all_to_all(jnp.stack(lax.axis_size('ctx') * [x_part], axis=0), 'ctx',...]
    reduce_sum x1, other arithmetic: 9.87 us -> 2.62 us  [per_device(): jnp.sum(jnp.where((lags >= 0)[:, :, None, None], terms, 0.0), axis=1)]
    dot_general x1, matrix products: 8.44 us -> 2.82 us  [per_device(): jnp.einsum('kn,anc->akc', forward[:, :SPAN], blocks, preferred_element_ty...]
    slice x2 -> x1, local copies, waits for them, and re-layouts: 5.23 us -> 0.2 us  [per_device(): blocks[:-1]]
  transfers between devices with their start and end apart: 3 -> 3, of which waited for: 3 -> 2; matrix products, arithmetic and copies ran while one was open for 10% -> 21% of each run, Pallas kernels for 0% -> 0%
where the time goes in v1:
time: 243 us; the launch traced here: 242 us
  waiting for transfers between devices  122 us (50%)
  other arithmetic  41.7 us (17%)
  local copies, waits for them, and re-layouts  33.7 us (14%)
  matrix products  22.9 us (9%)
  between operations  14.9 us (6%)
  starting transfers between devices  7.55 us (3%)
    all_gather x1, waiting for transfers between devices, per_device(): lax.all_gather(mixed, 'ch', axis=1, tiled=True)  89.3 us
    all_to_all x1, waiting for transfers between devices, per_device(): lax.all_to_all(jnp.stack(lax.axis_size('ctx') * [x_part], axis=0), 'ctx',...  32.4 us
    select_n x1, other arithmetic, per_device(): picked = jnp.take(seg_spec, jnp.maximum(lags, 0), axis=0)  17.5 us
    gather x1, local copies, waits for them, and re-layouts, per_device(): picked = jnp.take(seg_spec, jnp.maximum(lags, 0), axis=0)  15.2 us
    select_n x1, other arithmetic, spectral_product(): jnp.where(first, left_re * right_re, left_re * right_re - left_im * right...  11.9 us
    mul x2, local copies, waits for them, and re-layouts, spectral_product(): left_re * right_re  9.5 us
    dot_general x1, matrix products, per_device(): jnp.dot(lax.all_gather(mixed, 'ch', axis=1, tiled=True), w_out, preferred...  7.6 us
    all_to_all x1, starting transfers between devices, per_device(): lax.all_to_all(jnp.stack(lax.axis_size('ctx') * [x_part], axis=0), 'ctx',...  7.47 us
  transfers between devices with their start and end apart: 3, of which 2 were waited for; matrix products, arithmetic and copies ran while one was open for 21% of the time, Pallas kernels for 0%

profile of v1, /device:TPU:1, one launch (start us, length us, event | category | flops | bytes accessed | tf_op | source)
XLA Modules:
  0.0 242.5 jit_solution(4266550316189653021)
XLA Ops:
  7.2 1.2 convert_element_type.55
  8.4 1.9 stack.2
  10.3 7.5 %all-to-all-start = ((bf16[8,768,256]{2,1,0:T(8,128)(2,1)}), bf16[8,768,256]{2,1,0:T(8,128)(2,1)S(1)}, u32[]{:S(2)}, u32[]{:S(2)}) async-start(bf16[8,768,256]{2,1,0:T(8,128)(2,1)} %stack.2), calls=%async_computation | async-start | bytes 6291456 | tf_op jit(solution)/shard_map/all_to_all | solution.py:57
  17.8 1.7 multiply_convert_fusion
  19.7 0.6 dynamic_slice.8
  21.1 0.1 reshape.107
  21.2 5.7 %select_convert_fusion = bf16[512,512]{1,0:T(8,128)(2,1)} fusion(s32[512]{0:T(512)S(1)} %get-tuple-element.8, s32[512]{0:T(512)S(1)} %get-tuple-element.9, s32[512]{0:T(512)S(1)} %get-tuple-element.12, s32[512]{0:T(512)S(1)} %get-tuple-element.13, pred[512]{0:T(512)(128)(4,1)S(1)} %get-tuple-element.15, pred[512]{0:T(512)(128)(4,1)S(1)} %get-tuple-element.10, ...), kind=kLoop, calls=%fused_computation.21 | loop fusion | flops 6029312 | bytes 534528 | tf_op jit(solution)/shard_map/convert_element_type | solution.py:53
  27.0 32.4 %all-to-all-done = bf16[8,768,256]{2,1,0:T(8,128)(2,1)S(1)} async-done(((bf16[8,768,256]{2,1,0:T(8,128)(2,1)}), bf16[8,768,256]{2,1,0:T(8,128)(2,1)S(1)}, u32[]{:S(2)}, u32[]{:S(2)}) %all-to-all-start) | async-done | bytes 3145760 | tf_op jit(solution)/shard_map/all_to_all | solution.py:57
  59.4 0.2 slice.46
  59.6 2.8 %fusion.44 = f32[512,24,256]{2,0,1:T(8,128)S(1)} fusion(bf16[24,256,256]{2,1,0:T(8,128)(2,1)S(1)} %bitcast.44, bf16[512,512]{1,0:T(8,128)(2,1)} %select_convert_fusion), kind=kOutput, calls=%fused_computation.69 | convolution fusion | flops 1610612736 | bytes 15990784 | tf_op jit(solution)/shard_map/kn,anc->akc/dot_general | solution.py:62
  62.4 6.6 %bitcast_add_fusion = f32[24,512,256]{2,1,0:T(8,128)} fusion(f32[512,24,256]{2,0,1:T(8,128)S(1)} %fusion.44, bf16[23,256,256]{2,1,0:T(8,128)(2,1)S(1)} %slice.46, bf16[512,512]{1,0:T(8,128)(2,1)S(1)} %copy-done.1), kind=kOutput, calls=%fused_computation.4 | convolution fusion | flops 1607467008 | bytes 28442624 | tf_op jit(solution)/shard_map/kn,anc->akc/dot_general | solution.py:64
  69.0 15.2 %gather_fusion = f32[48,512,256]{2,1,0:T(8,128)} fusion(f32[24,512,256]{2,1,0:T(8,128)} %bitcast_add_fusion, s32[1024]{0:T(1024)S(1)} %pad_clamp_fusion), kind=kCustom, calls=%fused_computation | custom fusion | bytes 50331840 | tf_op jit(solution)/shard_map/jit(_take)/gather | solution.py:78
  84.2 17.5 %broadcast_select_fusion = f32[3,16,512,256]{3,2,1,0:T(8,128)} fusion(f32[3,16,512,256]{3,2,1,0:T(8,128)} %bitcast.42, pred[3,16]{1,0:T(4,128)(4,1)S(1)} %get-tuple-element.7), kind=kLoop, calls=%fused_computation.6 | loop fusion | flops 6291456 | bytes 50331696 | tf_op jit(solution)/shard_map/jit(_take)/select_n | solution.py:78
  101.7 2.9 %convolution_bitcast_fusion = f32[1,16,512,256]{2,3,1,0:T(8,128)S(1)} fusion(bf16[16,256,256]{2,1,0:T(8,128)(2,1)} %bitcast.45, bf16[512,512]{1,0:T(8,128)(2,1)S(1)} %copy-done.2), kind=kOutput, calls=%fused_computation.10 | convolution fusion | flops 1073741824 | bytes 10747904 | tf_op jit(solution)/shard_map/kn,anc->akc/dot_general | solution.py:68
  104.6 4.1 %slice_bitcast_fusion.1 = (f32[16,256,256]{1,2,0:T(8,128)}, f32[16,256,256]{1,2,0:T(8,128)}) fusion(f32[1,16,512,256]{2,3,1,0:T(8,128)S(1)} %convolution_bitcast_fusion), kind=kLoop, calls=%fused_computation.9 | loop fusion | bytes 16777216 | tf_op jit(solution)/shard_map/mul | solution.py:39
  108.8 5.4 %copy.17 = f32[16,256,256]{2,1,0:T(8,128)} copy(f32[16,256,256]{1,2,0:T(8,128)} %get-tuple-element.4) | data formatting | bytes 8388608 | tf_op jit(solution)/shard_map/mul | solution.py:39
  114.1 5.4 %copy.18 = f32[16,256,256]{2,1,0:T(8,128)} copy(f32[16,256,256]{1,2,0:T(8,128)} %get-tuple-element.5) | data formatting | bytes 8388608 | tf_op jit(solution)/shard_map/mul | solution.py:39
  119.5 11.9 %subtract_select_fusion = (f32[3,16,256,256]{3,2,1,0:T(8,128)S(1)}, f32[3,16,256,256]{3,2,1,0:T(8,128)S(1)}) fusion(f32[3,16,512,256]{3,2,1,0:T(8,128)} %broadcast_select_fusion, f32[16,256,256]{2,1,0:T(8,128)} %copy.18, f32[16,256,256]{2,1,0:T(8,128)} %copy.17, pred[256]{0:T(512)(128)(4,1)S(1)} %iota_compare_fusion.2), kind=kLoop, calls=%fused_computation.3 | loop fusion | flops 25165824 | bytes 58720512 | tf_op jit(solution)/shard_map/jit(_where)/select_n | solution.py:39
  131.4 2.6 %fusion = f32[3,512,256]{2,1,0:T(8,128)S(1)} fusion(f32[3,16,256,256]{3,2,1,0:T(8,128)S(1)} %get-tuple-element.3, f32[3,16,256,256]{3,2,1,0:T(8,128)S(1)} %get-tuple-element.2, pred[3,16]{1,0:T(4,128)(4,1)S(1)} %get-tuple-element.6), kind=kLoop, calls=%fused_computation.2 | loop fusion | flops 18481152 | bytes 26738736 | tf_op jit(solution)/shard_map/reduce_sum | solution.py:80
  134.1 3.0 %convolution_bitcast_fusion.1 = f32[3,256,256]{2,1,0:T(8,128)S(1)} fusion(f32[3,512,256]{2,1,0:T(8,128)S(1)} %fusion, s32[512]{0:T(512)S(1)} %get-tuple-element.8, s32[512]{0:T(512)S(1)} %get-tuple-element.9, s32[256]{0:T(256)S(1)} %get-tuple-element.16, s32[256]{0:T(256)S(1)} %get-tuple-element.17, pred[256]{0:T(512)(128)(4,1)S(1)} %compare_and_fusion, ...), kind=kOutput, calls=%fused_computation.16 | convolution fusion | flops 607518720 | bytes 2367232 | tf_op jit(solution)/shard_map/nk,akc->anc/dot_general | solution.py:81
  137.1 0.8 fusion.16
  138.0 0.7 slice_bitcast_fusion.2
  138.7 89.3 %all-gather.5.cloned.1.call-done = bf16[512,8192]{1,0:T(8,128)(2,1)} async-done(((bf16[512,256]{1,0:T(8,128)(2,1)}), bf16[512,8192]{1,0:T(8,128)(2,1)}) %all-gather.5.cloned.1.call-update) | async-done | bytes 8388624 | tf_op jit(solution)/shard_map/all_gather | solution.py:90
  228.0 7.6 %convolution_convert_fusion = bf16[512,256]{1,0:T(8,128)(2,1)} fusion(bf16[512,8192]{1,0:T(8,128)(2,1)} %all-gather.5.cloned.1.call-done, bf16[8192,256]{1,0:T(8,128)(2,1)} %param.13), kind=kOutput, calls=%fused_computation.17 | convolution fusion | flops 2147614720 | bytes 12845056 | tf_op jit(solution)/shard_map/dot_general | solution.py:89
  (34 shorter events, 0.5 us)
Async XLA Ops:
  7.2 10.6 %copy-start.3 = (bf16[512,256]{1,0:T(8,128)(2,1)S(1)}, bf16[512,256]{1,0:T(8,128)(2,1)}, u32[]{:S(2)}) copy-start(bf16[512,256]{1,0:T(8,128)(2,1)} %param.10) | copy-start | bytes 786436
  7.2 12.4 %copy-start.5 = (s32[16]{0:T(128)S(1)}, s32[16]{0:T(128)}, u32[]{:S(2)}) copy-start(s32[16]{0:T(128)} %param.14) | copy-start | bytes 196
  7.2 12.5 %copy-start.7 = (s32[8]{0:T(128)S(1)}, s32[8]{0:T(128)}, u32[]{:S(2)}) copy-start(s32[8]{0:T(128)} %param.15) | copy-start | bytes 100
  10.3 49.1 %all-to-all-start = ((bf16[8,768,256]{2,1,0:T(8,128)(2,1)}), bf16[8,768,256]{2,1,0:T(8,128)(2,1)S(1)}, u32[]{:S(2)}, u32[]{:S(2)}) async-start(bf16[8,768,256]{2,1,0:T(8,128)(2,1)} %stack.2), calls=%async_computation | async-start | bytes 6291456 | tf_op jit(solution)/shard_map/all_to_all | solution.py:57
  17.7 84.0 %all-gather.3.cloned.1.call-start = ((), (), s32[]{:S(2)}) async-start(), calls=%async_computation.1 | async-start | bytes 2359296 | tf_op jit(solution)/shard_map/all_gather | solution.py:67
  19.5 208.5 %all-gather.5.cloned.1.call-start = ((), (), s32[]{:S(2)}) async-start(), calls=%async_computation.2 | async-start | bytes 8650752 | tf_op jit(solution)/shard_map/all_gather | solution.py:90
  59.6 2.8 %copy-start.1 = (bf16[512,512]{1,0:T(8,128)(2,1)S(1)}, bf16[512,512]{1,0:T(8,128)(2,1)}, u32[]{:S(2)}) copy-start(bf16[512,512]{1,0:T(8,128)(2,1)} %select_convert_fusion) | copy-start | bytes 1572868
  84.2 17.5 %copy-start.2 = (bf16[512,512]{1,0:T(8,128)(2,1)S(1)}, bf16[512,512]{1,0:T(8,128)(2,1)}, u32[]{:S(2)}) copy-start(bf16[512,512]{1,0:T(8,128)(2,1)} %select_convert_fusion) | copy-start | bytes 1572868
  131.4 5.7 %copy-start = (bf16[512,256]{1,0:T(8,128)(2,1)S(1)}, bf16[512,256]{1,0:T(8,128)(2,1)}, u32[]{:S(2)}) copy-start(bf16[512,256]{1,0:T(8,128)(2,1)} %multiply_convert_fusion) | copy-start | bytes 786436
  131.4 5.7 %copy-start.4 = (bf16[512,256]{1,0:T(8,128)(2,1)S(1)}, bf16[512,256]{1,0:T(8,128)(2,1)}, u32[]{:S(2)}) copy-start(bf16[512,256]{1,0:T(8,128)(2,1)} %param.8) | copy-start | bytes 786436
  131.4 5.7 %copy-start.6 = (f32[256]{0:T(256)S(1)}, f32[256]{0:T(256)}, u32[]{:S(2)}) copy-start(f32[256]{0:T(256)} %param.12) | copy-start | bytes 3076
Sparse Core Ops, SparseCore 0:
  21.8 73.8 all-gather.2
  138.1 89.8 all-gather.4
